TPU v7x, 128 devices: a whole 4x4x4 slice. The times are simulated.
128 devices in a mesh: img: 8 (over z_hi, y), cap: 16 (over x, z_lo, core).
Axes of the slice: x: 4, y: 4, z: 4 (z_hi: 2, z_lo: 2; z = z_hi * 2 + z_lo), core: 2. Of those that a mesh axis runs over, the one named last changes fastest.
Arguments:
- images: float32 [16384, 768], P('img'), may hold values from -100 to 100
- captions: float32 [16384, 768], P('cap', 'img'), may hold values from -8 to 8
- bank: float32 [16384, 768], P('img'), may hold values from -100 to 100
Outputs:
- expected: float32 [16384, 768], P('img')
All inputs are finite; a program needn't handle non-finite values.
Results may differ from a plain program's by a relative error of at most 0.0003.
Values sent between devices are 32-bit elements; how exact they have to be, the bound alone decides.
No kernel may reach another device: no remote copies, remote signals or barrier semaphores. Data moves between devices by JAX's collectives and lax.ppermute only.
A program may use at most 448 MiB of HBM per device.

v0:
```python
import jax
import jax.numpy as jnp
from jax import lax
from jax.sharding import PartitionSpec as P

exponent_divisor = 0.03


def similar(query_factor, target_factor):
    return exponent_divisor * lax.dot_general(
        query_factor,
        target_factor,
        (((1,), (1,)), ((), ())),
        precision=lax.Precision.HIGHEST,
        preferred_element_type=jnp.float32,
    )


def rescaled_affinity(weights, features):
    return jnp.dot(
        weights, features, precision=lax.Precision.HIGHEST, preferred_element_type=jnp.float32
    )


def local(images, captions, bank):
    features = lax.all_gather(captions, "img", axis=1, tiled=True)
    querybank_similarity = similar(bank, features)
    local_peak = jnp.max(querybank_similarity, axis=0)
    peak = lax.pmax(local_peak, "img")
    total = lax.psum(jnp.sum(jnp.exp(querybank_similarity - peak[None, :]), axis=0), "img")
    col_log = peak + jnp.log(total)
    logits = similar(images, features) - col_log[None, :]
    row_peak = jnp.max(logits, axis=1)
    top = lax.pmax(row_peak, "cap")
    weights = jnp.exp(logits - top[:, None])
    summed, row_total = lax.psum(
        (rescaled_affinity(weights, features), jnp.sum(weights, axis=1)), "cap"
    )
    result = summed / row_total[:, None]
    return result


def solution(mesh):
    return jax.shard_map(
        local,
        mesh=mesh,
        in_specs=(P("img", None), P("cap", "img"), P("img", None)),
        out_specs=P("img", None),
        check_vma=False,
    )
```

profile of v0, /device:TPU:5, one launch (start us, length us, event | category | flops | bytes accessed | tf_op | source)
XLA Modules:
  0.0 408.6 jit_solution(2662504765495585626)
XLA Ops:
  6.5 0.0 all-gather.2.cloned.1.call-start
  6.5 0.7 all-gather.2.cloned.1.call-update
  7.3 0.0 all-reduce.2.cloned.1.call-start
  7.3 67.5 %all-gather.2.cloned.1.call-done = f32[1024,768]{0,1:T(8,128)} async-done(((f32[1024,96]{0,1:T(8,128)}), f32[1024,768]{0,1:T(8,128)}) %all-gather.2.cloned.1.call-update) | async-done | bytes 3145744 | tf_op jit(solution)/shard_map/all_gather | solution.py:26
  74.8 25.2 %multiply_reduce_fusion = (f32[1024]{0:T(1024)S(1)}, f32[2048,1024]{0,1:T(8,128)}) fusion(f32[2048,768]{1,0:T(8,128)} %param.5, f32[1024,768]{0,1:T(8,128)} %all-gather.2.cloned.1.call-done), kind=kOutput, calls=%fused_computation.3 | convolution fusion | flops 19331547136 | bytes 17829888 | tf_op jit(solution)/shard_map/dot_general | solution.py:10
  100.0 0.0 copy-start
  100.0 16.3 %pmax.14 = f32[1024]{0:T(1024)S(1)} all-reduce(f32[1024]{0:T(1024)S(1)} %get-tuple-element.5), channel_id=1, replica_groups=mesh['img'=8,'cap'=16] {'img'}, use_global_device_ids=true, to_apply=%region_1.0 | all-reduce | flops 1024 | bytes 8192 | tf_op jit(solution)/shard_map/pmax | solution.py:29
  116.3 4.4 %exponential_reduce_fusion = f32[1024]{0:T(1024)S(1)} fusion(f32[2048,1024]{0,1:T(8,128)} %get-tuple-element.6, f32[1024]{0:T(1024)S(1)} %pmax.14), kind=kLoop, calls=%fused_computation.1 | loop fusion | flops 6290432 | bytes 8396800 | tf_op jit(solution)/shard_map/reduce_sum | solution.py:30
  120.7 16.5 %psum.21 = f32[1024]{0:T(1024)S(1)} all-reduce(f32[1024]{0:T(1024)S(1)} %exponential_reduce_fusion), channel_id=1, replica_groups=mesh['img'=8,'cap'=16] {'img'}, use_global_device_ids=true, to_apply=%region_3.0 | all-reduce | flops 1024 | bytes 8192 | tf_op jit(solution)/shard_map/psum | solution.py:30
  137.2 0.0 copy-done
  137.2 25.1 %fusion = (f32[2048]{0:T(1024)S(1)}, f32[2048,1024]{0,1:T(8,128)}) fusion(f32[1024]{0:T(1024)S(1)} %log_add_fusion, f32[2048,768]{1,0:T(8,128)} %param.3, f32[1024,768]{0,1:T(8,128)S(1)} %copy-done), kind=kOutput, calls=%fused_computation.4 | convolution fusion | flops 19333642240 | bytes 17838080 | tf_op jit(solution)/shard_map/dot_general | solution.py:10
  162.4 30.7 %pmax.15 = f32[2048]{0:T(1024)S(1)} all-reduce(f32[2048]{0:T(1024)S(1)} %get-tuple-element.7), channel_id=1, replica_groups=mesh['img'=8,'cap'=16] {'cap'}, use_global_device_ids=true, to_apply=%region_5.0 | all-reduce | flops 2048 | bytes 16384 | tf_op jit(solution)/shard_map/pmax | solution.py:34
  193.1 44.3 %fusion.2 = f32[2048,768]{1,0:T(8,128)} fusion(f32[1024,768]{0,1:T(8,128)S(1)} %copy-done, f32[2048,1024]{0,1:T(8,128)} %get-tuple-element.8, f32[2048]{0:T(1024)S(1)} %pmax.15, f32[1024]{0:T(1024)S(1)} %log_add_fusion), kind=kOutput, calls=%fused_computation.6 | convolution fusion | flops 19333644288 | bytes 17838080 | tf_op jit(solution)/shard_map/dot_general | solution.py:20
  237.5 0.0 all-reduce.2.cloned.1.call-update
  237.5 4.5 %fusion.1 = f32[2048]{0:T(1024)S(1)} fusion(f32[2048,1024]{0,1:T(8,128)} %get-tuple-element.8, f32[2048]{0:T(1024)S(1)} %pmax.15, f32[1024]{0:T(1024)S(1)} %log_add_fusion), kind=kLoop, calls=%fused_computation.5 | loop fusion | flops 8386560 | bytes 8409088 | tf_op jit(solution)/shard_map/reduce_sum | solution.py:37
  242.0 23.2 %psum.23 = f32[2048]{0:T(1024)S(1)} all-reduce(f32[2048]{0:T(1024)S(1)} %fusion.1), channel_id=1, replica_groups=mesh['img'=8,'cap'=16] {'cap'}, use_global_device_ids=true, to_apply=%region_8.0 | all-reduce | flops 2048 | bytes 16384 | tf_op jit(solution)/shard_map/psum | solution.py:36
  265.2 130.2 %all-reduce.2.cloned.1.call-done = f32[2048,768]{1,0:T(8,128)} async-done(((f32[2048,768]{1,0:T(8,128)}), f32[2048,768]{1,0:T(8,128)}) %all-reduce.2.cloned.1.call-update) | async-done | bytes 6291472 | tf_op jit(solution)/shard_map/psum | solution.py:36
  395.4 6.0 %broadcast_divide_fusion = f32[2048,768]{1,0:T(8,128)} fusion(f32[2048,768]{1,0:T(8,128)} %all-reduce.2.cloned.1.call-done, f32[2048]{0:T(1024)S(1)} %psum.23), kind=kLoop, calls=%fused_computation.10 | loop fusion | flops 1572864 | bytes 12591104 | tf_op jit(solution)/shard_map/div | solution.py:39
  (1 shorter events, 0.0 us)
Async XLA Ops:
  6.5 68.3 %all-gather.2.cloned.1.call-start = ((), (), s32[]{:S(2)}) async-start(), calls=%async_computation | async-start | bytes 3538944 | tf_op jit(solution)/shard_map/all_gather | solution.py:26
  7.3 388.2 %all-reduce.2.cloned.1.call-start = ((), (), s32[]{:S(2)}) async-start(), calls=%async_computation.1 | async-start | bytes 12582912 | tf_op jit(solution)/shard_map/psum | solution.py:36
  100.0 37.2 %copy-start = (f32[1024,768]{0,1:T(8,128)S(1)}, f32[1024,768]{0,1:T(8,128)}, u32[]{:S(2)}) copy-start(f32[1024,768]{0,1:T(8,128)} %all-gather.2.cloned.1.call-done) | copy-start | bytes 9437188
Sparse Core Ops, SparseCore 0:
  9.7 65.0 all-gather.1
  237.6 157.7 all-reduce.1
where the time goes:
time: 417 us; the launch traced here: 409 us
  waiting for transfers between devices  198 us (47%)
  matrix products  94.7 us (23%)
  blocking collectives  86.8 us (21%)
  other arithmetic  14.9 us (4%)
  between operations  13.8 us (3%)
    psum x1, waiting for transfers between devices, local(): lax.psum((rescaled_affinity(weights, features), jnp.sum(weights, axis=1))...  130 us
    all_gather x1, waiting for transfers between devices, local(): features = lax.all_gather(captions, 'img', axis=1, tiled=True)  67.5 us
    dot_general x2, matrix products, similar(): lax.dot_general(query_factor, target_factor, (((1,), (1,)), ((), ())), pr...  50.4 us
    dot_general x1, matrix products, rescaled_affinity(): jnp.dot(weights, features, precision=lax.Precision.HIGHEST, preferred_ele...  44.3 us
    pmax x1, blocking collectives, local(): top = lax.pmax(row_peak, 'cap')  30.7 us
    psum x1, blocking collectives, local(): lax.psum((rescaled_affinity(weights, features), jnp.sum(weights, axis=1))...  23.2 us
    psum x1, blocking collectives, local(): lax.psum(jnp.sum(jnp.exp(querybank_similarity - peak[None, :]), axis=0),...  16.5 us
    pmax x1, blocking collectives, local(): peak = lax.pmax(local_peak, 'img')  16.3 us
  transfers between devices with their start and end apart: 2, of which 2 were waited for; matrix products, arithmetic and copies ran while one was open for 1% of the time, Pallas kernels for 0%

commit v1 on v0

--- a/solution.py
+++ b/solution.py
@@ -4,6 +4,12 @@
 from jax.sharding import PartitionSpec as P
 
 exponent_divisor = 0.03
+
+
+def gather_and_add(block, axis):
+    parts = lax.all_gather(block, axis, axis=0, tiled=False)
+    total = parts.sum(axis=0)
+    return total
 
 
 def similar(query_factor, target_factor):
@@ -27,7 +33,7 @@
     querybank_similarity = similar(bank, features)
     local_peak = jnp.max(querybank_similarity, axis=0)
     peak = lax.pmax(local_peak, "img")
-    total = lax.psum(jnp.sum(jnp.exp(querybank_similarity - peak[None, :]), axis=0), "img")
+    total = gather_and_add(jnp.sum(jnp.exp(querybank_similarity - peak[None, :]), axis=0), "img")
     col_log = peak + jnp.log(total)
     logits = similar(images, features) - col_log[None, :]
     row_peak = jnp.max(logits, axis=1)

time: 417 us -> 430 us (1.031)
  blocking collectives: 86.8 us -> 103 us
    all_gather x0 -> x1, blocking collectives: none -> 27.7 us  [gather_and_add(): parts = lax.all_gather(block, axis, axis=0, tiled=False)]
    psum x1 -> x0, blocking collectives: 16.5 us -> none  [local(): lax.psum(jnp.sum(jnp.exp(querybank_similarity - peak[None, :]), axis=0),...]
where the time goes in v1:
time: 430 us; the launch traced here: 422 us
  waiting for transfers between devices  196 us (46%)
  blocking collectives  103 us (24%)
  matrix products  94.7 us (22%)
  other arithmetic  14.9 us (3%)
  between operations  13.8 us (3%)
    psum x1, waiting for transfers between devices, local(): lax.psum((rescaled_affinity(weights, features), jnp.sum(weights, axis=1))...  128 us
    all_gather x1, waiting for transfers between devices, local(): features = lax.all_gather(captions, 'img', axis=1, tiled=True)  67.5 us
    dot_general x2, matrix products, similar(): lax.dot_general(query_factor, target_factor, (((1,), (1,)), ((), ())), pr...  50.3 us
    dot_general x1, matrix products, rescaled_affinity(): jnp.dot(weights, features, precision=lax.Precision.HIGHEST, preferred_ele...  44.3 us
    pmax x1, blocking collectives, local(): top = lax.pmax(row_peak, 'cap')  34.5 us
    all_gather x1, blocking collectives, gather_and_add(): parts = lax.all_gather(block, axis, axis=0, tiled=False)  27.7 us
    psum x1, blocking collectives, local(): lax.psum((rescaled_affinity(weights, features), jnp.sum(weights, axis=1))...  24 us
    pmax x1, blocking collectives, local(): peak = lax.pmax(local_peak, 'img')  16.3 us
  transfers between devices with their start and end apart: 2, of which 2 were waited for; matrix products, arithmetic and copies ran while one was open for 1% of the time, Pallas kernels for 0%

profile of v1, /device:TPU:5, one launch (start us, length us, event | category | flops | bytes accessed | tf_op | source)
XLA Modules:
  0.0 421.9 jit_solution(16876786846377444876)
XLA Ops:
  6.5 0.0 all-gather.3.cloned.1.call-start
  6.5 0.7 all-gather.3.cloned.1.call-update
  7.3 0.0 all-reduce.2.cloned.1.call-start
  7.3 67.5 %all-gather.3.cloned.1.call-done = f32[1024,768]{0,1:T(8,128)} async-done(((f32[1024,96]{0,1:T(8,128)}), f32[1024,768]{0,1:T(8,128)}) %all-gather.3.cloned.1.call-update) | async-done | bytes 3145744 | tf_op jit(solution)/shard_map/all_gather | solution.py:32
  74.8 25.2 %multiply_reduce_fusion = (f32[1024]{0:T(1024)S(1)}, f32[2048,1024]{0,1:T(8,128)}) fusion(f32[2048,768]{1,0:T(8,128)} %param.5, f32[1024,768]{0,1:T(8,128)} %all-gather.3.cloned.1.call-done), kind=kOutput, calls=%fused_computation.3 | convolution fusion | flops 19331547136 | bytes 17829888 | tf_op jit(solution)/shard_map/dot_general | solution.py:16
  100.0 0.0 copy-start
  100.0 16.3 %pmax.14 = f32[1024]{0:T(1024)S(1)} all-reduce(f32[1024]{0:T(1024)S(1)} %get-tuple-element.5), channel_id=1, replica_groups=mesh['img'=8,'cap'=16] {'img'}, use_global_device_ids=true, to_apply=%region_1.0 | all-reduce | flops 1024 | bytes 8192 | tf_op jit(solution)/shard_map/pmax | solution.py:35
  116.3 4.4 %exponential_reduce_fusion = f32[1024]{0:T(1024)S(1)} fusion(f32[2048,1024]{0,1:T(8,128)} %get-tuple-element.6, f32[1024]{0:T(1024)S(1)} %pmax.14), kind=kLoop, calls=%fused_computation.1 | loop fusion | flops 6290432 | bytes 8396800 | tf_op jit(solution)/shard_map/reduce_sum | solution.py:36
  120.7 27.7 %all-gather = f32[8192]{0:T(1024)S(1)} all-gather(f32[1024]{0:T(1024)S(1)} %exponential_reduce_fusion), channel_id=2, replica_groups=mesh['img'=8,'cap'=16] {'img'}, dimensions={0}, use_global_device_ids=true | all-gather | bytes 36864 | tf_op jit(solution)/shard_map/all_gather | solution.py:10
  148.5 0.0 copy-done
  148.5 25.1 %fusion = (f32[2048]{0:T(1024)S(1)}, f32[2048,1024]{0,1:T(8,128)}) fusion(f32[1024]{0:T(1024)S(1)} %log_add_fusion, f32[2048,768]{1,0:T(8,128)} %param.3, f32[1024,768]{0,1:T(8,128)S(1)} %copy-done), kind=kOutput, calls=%fused_computation.4 | convolution fusion | flops 19333642240 | bytes 17838080 | tf_op jit(solution)/shard_map/dot_general | solution.py:16
  173.6 34.5 %pmax.15 = f32[2048]{0:T(1024)S(1)} all-reduce(f32[2048]{0:T(1024)S(1)} %get-tuple-element.7), channel_id=1, replica_groups=mesh['img'=8,'cap'=16] {'cap'}, use_global_device_ids=true, to_apply=%region_5.0 | all-reduce | flops 2048 | bytes 16384 | tf_op jit(solution)/shard_map/pmax | solution.py:40
  208.1 44.3 %fusion.2 = f32[2048,768]{1,0:T(8,128)} fusion(f32[1024,768]{0,1:T(8,128)S(1)} %copy-done, f32[2048,1024]{0,1:T(8,128)} %get-tuple-element.8, f32[2048]{0:T(1024)S(1)} %pmax.15, f32[1024]{0:T(1024)S(1)} %log_add_fusion), kind=kOutput, calls=%fused_computation.6 | convolution fusion | flops 19333644288 | bytes 17838080 | tf_op jit(solution)/shard_map/dot_general | solution.py:26
  252.4 0.0 all-reduce.2.cloned.1.call-update
  252.4 4.5 %fusion.1 = f32[2048]{0:T(1024)S(1)} fusion(f32[2048,1024]{0,1:T(8,128)} %get-tuple-element.8, f32[2048]{0:T(1024)S(1)} %pmax.15, f32[1024]{0:T(1024)S(1)} %log_add_fusion), kind=kLoop, calls=%fused_computation.5 | loop fusion | flops 8386560 | bytes 8409088 | tf_op jit(solution)/shard_map/reduce_sum | solution.py:43
  257.0 24.0 %psum.15 = f32[2048]{0:T(1024)S(1)} all-reduce(f32[2048]{0:T(1024)S(1)} %fusion.1), channel_id=1, replica_groups=mesh['img'=8,'cap'=16] {'cap'}, use_global_device_ids=true, to_apply=%region_8.0 | all-reduce | flops 2048 | bytes 16384 | tf_op jit(solution)/shard_map/psum | solution.py:42
  281.0 127.7 %all-reduce.2.cloned.1.call-done = f32[2048,768]{1,0:T(8,128)} async-done(((f32[2048,768]{1,0:T(8,128)}), f32[2048,768]{1,0:T(8,128)}) %all-reduce.2.cloned.1.call-update) | async-done | bytes 6291472 | tf_op jit(solution)/shard_map/psum | solution.py:42
  408.7 6.0 %broadcast_divide_fusion = f32[2048,768]{1,0:T(8,128)} fusion(f32[2048,768]{1,0:T(8,128)} %all-reduce.2.cloned.1.call-done, f32[2048]{0:T(1024)S(1)} %psum.15), kind=kLoop, calls=%fused_computation.10 | loop fusion | flops 1572864 | bytes 12591104 | tf_op jit(solution)/shard_map/div | solution.py:45
  (3 shorter events, 0.0 us)
Async XLA Ops:
  6.5 68.3 %all-gather.3.cloned.1.call-start = ((), (), s32[]{:S(2)}) async-start(), calls=%async_computation | async-start | bytes 3538944 | tf_op jit(solution)/shard_map/all_gather | solution.py:32
  7.3 401.5 %all-reduce.2.cloned.1.call-start = ((), (), s32[]{:S(2)}) async-start(), calls=%async_computation.1 | async-start | bytes 12582912 | tf_op jit(solution)/shard_map/psum | solution.py:42
  100.0 48.4 %copy-start = (f32[1024,768]{0,1:T(8,128)S(1)}, f32[1024,768]{0,1:T(8,128)}, u32[]{:S(2)}) copy-start(f32[1024,768]{0,1:T(8,128)} %all-gather.3.cloned.1.call-done) | copy-start | bytes 9437188
Sparse Core Ops, SparseCore 0:
  9.7 65.0 all-gather.2
  252.6 156.1 all-reduce.1
